TPU v7x, 256 devices: a whole 4x4x8 slice. The times are simulated.
256 devices in a mesh: grp: 4 (over y), mdl: 64 (over z, x, core).
Axes of the slice: x: 4, y: 4, z: 8, core: 2. Of those that a mesh axis runs over, the one named last changes fastest.
Arguments:
- pol_hidden: bfloat16 [1024, 4096], P(('grp', 'mdl')), may hold values from -6 to 6
- ref_hidden: bfloat16 [1024, 4096], P(('grp', 'mdl')), may hold values from -6 to 6
- pol_mlp_gain: bfloat16 [4096], replicated, may hold values from 0.099609375 to 1.8984375
- ref_mlp_gain: bfloat16 [4096], replicated, may hold values from 0.099609375 to 1.8984375
- pol_final_gain: bfloat16 [4096], replicated, may hold values from 0.099609375 to 1.8984375
- ref_final_gain: bfloat16 [4096], replicated, may hold values from 0.099609375 to 1.8984375
- pol_gate: bfloat16 [4096, 11008], P(None, 'mdl'), may hold values from -0.09375 to 0.09375
- pol_up: bfloat16 [4096, 11008], P(None, 'mdl'), may hold values from -0.09375 to 0.09375
- pol_down: bfloat16 [11008, 4096], P('mdl'), may hold values from -0.109375 to 0.109375
- ref_gate: bfloat16 [4096, 11008], P(None, 'mdl'), may hold values from -0.09375 to 0.09375
- ref_up: bfloat16 [4096, 11008], P(None, 'mdl'), may hold values from -0.09375 to 0.09375
- ref_down: bfloat16 [11008, 4096], P('mdl'), may hold values from -0.109375 to 0.109375
- pol_head: bfloat16 [64000, 4096], P(('grp', 'mdl')), may hold values from -20 to 20
- ref_head: bfloat16 [64000, 4096], P(('grp', 'mdl')), may hold values from -20 to 20
- token_ids: int32 [1024], replicated, may hold values from 0 to 63999
- lengths: int32 [16], replicated, may hold values from 1 to 160, 1024 in all
Outputs:
- pol_out: bfloat16 [1024, 4096], P(('grp', 'mdl'))
- ref_out: bfloat16 [1024, 4096], P(('grp', 'mdl'))
- rollout_ratio: float32 [16], replicated
Inputs may be any that keep to these rules, and one draw needn't show every extreme that they name: Rollout lengths sum to 1024; the longest is exactly 160.
All inputs are finite; a program needn't handle non-finite values.
Results may differ from a plain program's by a relative error of at most 0.012.
The roundings to bfloat16 on the way count: a program that leaves them out, or rounds other values in their place, can miss the bound.
Values may be sent and summed in bfloat16 or wider, within the bound.
No kernel may reach another device: no remote copies, remote signals or barrier semaphores. Data moves between devices by JAX's collectives and lax.ppermute only.
A program may use at most 128 MiB of HBM per device.

v0:
```python
import jax
import jax.numpy as jnp
from jax import lax
from jax.sharding import PartitionSpec as P


def rms_rows(rows, gain):
    values = rows.astype(jnp.float32)
    scale = lax.rsqrt(jnp.mean(values * values, axis=-1, keepdims=True) + 1e-05)
    return (values * scale * gain.astype(jnp.float32)).astype(jnp.bfloat16)


def mlp_partial(piece, gain, w_gate, w_up, w_down):
    normed = rms_rows(piece, gain)
    gate = jnp.dot(normed, w_gate, preferred_element_type=jnp.float32)
    upper = jnp.dot(normed, w_up, preferred_element_type=jnp.float32)
    hidden = (jax.nn.silu(gate) * upper).astype(jnp.bfloat16)
    return jnp.dot(hidden, w_down, preferred_element_type=jnp.float32)


def vocab_terms(token_rows, head_rows, targets, vocab):
    logits = jnp.einsum("td,vd->tv", token_rows, head_rows, preferred_element_type=jnp.float32)
    peak = jnp.max(logits, axis=1)
    total = jnp.sum(jnp.exp(logits - peak[:, None]), axis=1)
    target = jnp.sum(jnp.where(targets[:, None] == vocab[None, :], logits, 0.0), axis=1)
    return (peak, total, target)


def rollout_totals(log_ratio, positions, lengths):
    ends = jnp.cumsum(lengths)
    owner = jnp.sum((positions[:, None] >= ends[None, :]).astype(jnp.int32), axis=1)
    onehot = (owner[:, None] == jnp.arange(lengths.shape[0], dtype=jnp.int32)[None, :]).astype(
        jnp.float32
    )
    return jnp.sum(log_ratio[:, None] * onehot, axis=0)


def per_device(
    pol_hidden,
    ref_hidden,
    pol_mlp_gain,
    ref_mlp_gain,
    pol_final_gain,
    ref_final_gain,
    pol_gate,
    pol_up,
    pol_down,
    ref_gate,
    ref_up,
    ref_down,
    pol_head,
    ref_head,
    token_ids,
    lengths,
):
    rows = pol_hidden.shape[0]
    member = lax.axis_index("mdl")
    group = lax.axis_index("grp")
    members = lax.axis_size("mdl")
    both_in = lax.all_gather(jnp.stack([pol_hidden, ref_hidden]), "mdl", axis=1, tiled=True)
    partials = (
        mlp_partial(both_in[0], pol_mlp_gain, pol_gate, pol_up, pol_down),
        mlp_partial(both_in[1], ref_mlp_gain, ref_gate, ref_up, ref_down),
    )
    mixed = lax.psum(partials, "mdl")
    outs = [(both_in[i].astype(jnp.float32) + mixed[i]).astype(jnp.bfloat16) for i in range(2)]
    finals = jnp.stack([rms_rows(outs[0], pol_final_gain), rms_rows(outs[1], ref_final_gain)])
    own = [lax.dynamic_slice_in_dim(o, member * rows, rows, axis=0) for o in outs]
    every = lax.all_gather(finals, "grp", axis=1, tiled=True)
    voc_dev = pol_head.shape[0]
    positions = jnp.arange(every.shape[1], dtype=jnp.int32)
    vocab = (group * members + member) * voc_dev + jnp.arange(voc_dev, dtype=jnp.int32)
    pol_terms = vocab_terms(every[0], pol_head, token_ids, vocab)
    ref_terms = vocab_terms(every[1], ref_head, token_ids, vocab)
    peaks = lax.pmax(lax.pmax((pol_terms[0], ref_terms[0]), "mdl"), "grp")
    sums = lax.psum(
        lax.psum(
            (
                pol_terms[1] * jnp.exp(pol_terms[0] - peaks[0]),
                pol_terms[2],
                ref_terms[1] * jnp.exp(ref_terms[0] - peaks[1]),
                ref_terms[2],
            ),
            "mdl",
        ),
        "grp",
    )
    pol_logp = sums[1] - peaks[0] - jnp.log(sums[0])
    ref_logp = sums[3] - peaks[1] - jnp.log(sums[2])
    rollout_ratio = rollout_totals(pol_logp - ref_logp, positions, lengths)
    return (own[0], own[1], rollout_ratio)


def solution(mesh):
    placed = (
        P(("grp", "mdl"), None),
        P(("grp", "mdl"), None),
        P(),
        P(),
        P(),
        P(),
        P(None, "mdl"),
        P(None, "mdl"),
        P("mdl", None),
        P(None, "mdl"),
        P(None, "mdl"),
        P("mdl", None),
        P(("grp", "mdl"), None),
        P(("grp", "mdl"), None),
        P(),
        P(),
    )
    return jax.shard_map(
        per_device,
        mesh=mesh,
        in_specs=placed,
        out_specs=(P(("grp", "mdl"), None), P(("grp", "mdl"), None), P()),
        check_vma=False,
    )
```

profile of v0, /device:TPU:8, one launch (start us, length us, event | category | flops | bytes accessed | tf_op | source)
XLA Modules:
  0.0 921.6 jit_solution(18328997950964783200)
XLA Ops:
  7.2 1.0 pad_maximum_fusion.1
  9.0 1.3 convert_element_type.62
  11.0 81.7 %all-gather.3.cloned.1.call-done = bf16[2,256,4096]{2,0,1:T(2,128)(2,1)} async-done(((bf16[2,4,4096]{2,0,1:T(2,128)(2,1)}), bf16[2,256,4096]{2,0,1:T(2,128)(2,1)}) %all-gather.3.cloned.1.call-update) | async-done | bytes 4194320 | tf_op jit(solution)/shard_map/all_gather | solution.py:60
  92.7 13.2 %fusion.48 = (bf16[1,256,4096]{2,0,1:T(2,128)(2,1)S(1)}, bf16[1,256,4096]{2,0,1:T(2,128)(2,1)S(1)}) fusion(bf16[2,256,4096]{2,0,1:T(2,128)(2,1)} %all-gather.3.cloned.1.call-done), kind=kLoop, calls=%fused_computation.76 | loop fusion | bytes 8388608 | tf_op jit(solution)/shard_map/slice | solution.py:66
  105.9 6.7 fusion.8
  113.9 1.6 fusion.30
  115.5 6.6 fusion.21
  122.1 3.7 fusion.26
  125.8 6.6 fusion.20
  133.1 201.9 %all-reduce.7.cloned.1.call-done = (f32[256,4096]{1,0:T(8,128)}, f32[256,4096]{1,0:T(8,128)}) async-done(((f32[256,4096]{1,0:T(8,128)}, f32[256,4096]{1,0:T(8,128)}), (f32[256,4096]{1,0:T(8,128)}, f32[256,4096]{1,0:T(8,128)})) %all-reduce.7.cloned.1.call-update) | async-done | bytes 8388624 | tf_op jit(solution)/shard_map/psum | solution.py:65
  335.0 3.8 fusion.2
  339.7 0.8 fusion.5
  342.5 2.3 pad_maximum_fusion
  345.8 1.5 constant_dynamic-slice_fusion.1
  347.3 1.5 constant_dynamic-slice_fusion
  348.8 151.6 %all-gather.5.cloned.1.call-done = bf16[2,1024,4096]{2,1,0:T(8,128)(2,1)} async-done(((bf16[2,256,4096]{2,1,0:T(8,128)(2,1)}), bf16[2,1024,4096]{2,1,0:T(8,128)(2,1)}) %all-gather.5.cloned.1.call-update) | async-done | bytes 16777232 | tf_op jit(solution)/shard_map/all_gather | solution.py:69
  500.4 5.9 fusion.49
  506.3 2.2 copy-done.14
  509.2 3.4 fusion.50
  512.5 131.0 %all-reduce.2 = (f32[1024]{0:T(1024)S(1)}, f32[1024]{0:T(1024)S(1)}) all-reduce(f32[1024]{0:T(1024)S(1)} %get-tuple-element.35, f32[1024]{0:T(1024)S(1)} %get-tuple-element.33), channel_id=1, replica_groups=mesh['grp'=4,'mdl'=64] {'mdl'}, use_global_device_ids=true, to_apply=%region_21.22 | all-reduce | flops 2048 | bytes 16384 | tf_op jit(solution)/shard_map/pmax | solution.py:75
  643.5 8.4 all-reduce.4
  652.0 1.7 fusion.22
  653.7 246.2 %all-reduce = (f32[1024]{0:T(1024)S(1)}, f32[1024]{0:T(1024)S(1)}, f32[1024]{0:T(1024)S(1)}, f32[1024]{0:T(1024)S(1)}) all-reduce(f32[1024]{0:T(1024)S(1)} %exponential_multiply_fusion, f32[1024]{0:T(1024)S(1)} %get-tuple-element.8, f32[1024]{0:T(1024)S(1)} %exponential_multiply_fusion.1, ...), channel_id=1, replica_groups=mesh['grp'=4,'mdl'=64] {'mdl'}, use_global_device_ids=true, to_apply=%region_24.25 | all-reduce | flops 4096 | bytes 32768 | tf_op jit(solution)/shard_map/psum | solution.py:77
  899.9 14.6 %all-reduce.3 = (f32[1024]{0:T(1024)S(1)}, f32[1024]{0:T(1024)S(1)}, f32[1024]{0:T(1024)S(1)}, f32[1024]{0:T(1024)S(1)}) all-reduce(f32[1024]{0:T(1024)S(1)} %get-tuple-element.9, f32[1024]{0:T(1024)S(1)} %get-tuple-element.10, f32[1024]{0:T(1024)S(1)} %get-tuple-element.11, ...), channel_id=1, replica_groups=mesh['grp'=4,'mdl'=64] {'grp'}, use_global_device_ids=true, to_apply=%region_25.26 | all-reduce | flops 4096 | bytes 32768 | tf_op jit(solution)/shard_map/psum | solution.py:76
  (58 shorter events, 8.5 us)
Async XLA Ops:
  7.2 493.2 %copy-start = (bf16[250,4096]{1,0:T(8,128)(2,1)S(1)}, bf16[250,4096]{1,0:T(8,128)(2,1)}, u32[]{:S(2)}) copy-start(bf16[250,4096]{1,0:T(8,128)(2,1)} %param.28) | copy-start | bytes 6144004
  7.2 85.5 %all-gather.3.cloned.1.call-start = ((), (), s32[]{:S(2)}) async-start(), calls=%async_computation | async-start | bytes 4259840 | tf_op jit(solution)/shard_map/all_gather | solution.py:60
  8.9 326.1 %all-reduce.7.cloned.1.call-start = ((), (), s32[]{:S(2)}) async-start(), calls=%async_computation.2 | async-start | bytes 16777216 | tf_op jit(solution)/shard_map/psum | solution.py:65
  105.9 8.0 copy-start.8
  105.9 8.0 copy-start.16
  112.6 1.3 copy-start.2
  112.6 1.3 copy-start.12
  113.9 1.6 copy-start.6
  122.1 3.7 copy-start.7
  132.4 0.7 copy-start.9
  132.4 0.7 copy-start.10
  132.4 368.0 %all-gather.5.cloned.1.call-start = ((), (), s32[]{:S(2)}) async-start(), calls=%async_computation.1 | async-start | bytes 20971520 | tf_op jit(solution)/shard_map/all_gather | solution.py:69
  335.0 3.9 copy-start.1
  335.0 4.7 copy-start.5
  338.9 3.0 copy-start.3
  340.6 1.3 copy-start.4
  344.8 0.7 copy-start.13
  500.4 8.2 copy-start.14
  500.4 8.7 copy-start.15
  509.2 142.8 %copy-start.11 = (s32[1024]{0:T(1024)S(1)}, s32[1024]{0:T(1024)}, u32[]{:S(2)}) copy-start(s32[1024]{0:T(1024)} %param.30) | copy-start | bytes 12292
Sparse Core Ops, SparseCore 0:
  10.8 81.8 all-gather.2
  132.5 202.4 all-reduce.6
  345.0 155.3 all-gather.4
where the time goes:
time: 922 us
  waiting for transfers between devices  435 us (47%)
  blocking collectives  400 us (43%)
  matrix products  27.8 us (3%)
  local copies, waits for them, and re-layouts  23 us (2%)
  other arithmetic  21.2 us (2%)
  between operations  13.9 us (2%)
    psum x1, blocking collectives, per_device(): lax.psum((pol_terms[1] * jnp.exp(pol_terms[0] - peaks[0]), pol_terms[2],...  246 us
    psum x1, waiting for transfers between devices, per_device(): mixed = lax.psum(partials, 'mdl')  202 us
    all_gather x1, waiting for transfers between devices, per_device(): every = lax.all_gather(finals, 'grp', axis=1, tiled=True)  152 us
    pmax x2, blocking collectives, per_device(): peaks = lax.pmax(lax.pmax((pol_terms[0], ref_terms[0]), 'mdl'), 'grp')  139 us
    all_gather x1, waiting for transfers between devices, per_device(): lax.all_gather(jnp.stack([pol_hidden, ref_hidden]), 'mdl', axis=1, tiled=...  81.7 us
  transfers between devices with their start and end apart: 3, of which 3 were waited for; matrix products, arithmetic and copies ran while one was open for 1% of the time, Pallas kernels for 0%

commit v1 on v0

--- a/solution.py
+++ b/solution.py
@@ -2,6 +2,19 @@
 import jax.numpy as jnp
 from jax import lax
 from jax.sharding import PartitionSpec as P
+
+
+def gather_around(value, axis, dim):
+    ways = lax.axis_size(axis)
+    up = [(d, (d + 1) % ways) for d in range(ways)]
+    down = [(d, (d - 1) % ways) for d in range(ways)]
+    earlier, later = ([value], [value])
+    for _ in range(ways // 2):
+        earlier.append(lax.ppermute(earlier[-1], axis, up))
+    for _ in range((ways - 1) // 2):
+        later.append(lax.ppermute(later[-1], axis, down))
+    line = jnp.concatenate([*earlier[::-1], *later[1:]], axis=dim)
+    return jnp.roll(line, (lax.axis_index(axis) - ways // 2) * value.shape[dim], axis=dim)
 
 
 def rms_rows(rows, gain):
@@ -66,7 +79,7 @@
     outs = [(both_in[i].astype(jnp.float32) + mixed[i]).astype(jnp.bfloat16) for i in range(2)]
     finals = jnp.stack([rms_rows(outs[0], pol_final_gain), rms_rows(outs[1], ref_final_gain)])
     own = [lax.dynamic_slice_in_dim(o, member * rows, rows, axis=0) for o in outs]
-    every = lax.all_gather(finals, "grp", axis=1, tiled=True)
+    every = gather_around(finals, "grp", 1)
     voc_dev = pol_head.shape[0]
     positions = jnp.arange(every.shape[1], dtype=jnp.int32)
     vocab = (group * members + member) * voc_dev + jnp.arange(voc_dev, dtype=jnp.int32)

time: 922 us -> 985 us (1.068)
  local copies, waits for them, and re-layouts: 23 us -> 48.3 us
  waiting for transfers between devices: 435 us -> 459 us
    ppermute x0 -> x3, waiting for transfers between devices: none -> 175 us  [the longest x2 175 us: gather_around(): earlier.append(lax.ppermute(earlier[-1], axis, up))]
    all_gather x1 -> x0, waiting for transfers between devices: 152 us -> none  [per_device(): every = lax.all_gather(finals, 'grp', axis=1, tiled=True)]
    unnamed x34 -> x45, local copies, waits for them, and re-layouts: 6.11 us -> 26.7 us
  transfers between devices with their start and end apart: 3 -> 5, of which waited for: 3 -> 4; matrix products, arithmetic and copies ran while one was open for 1% -> 2% of each run, Pallas kernels for 0% -> 0%
where the time goes in v1:
time: 985 us; the launch traced here: 984 us
  waiting for transfers between devices  459 us (47%)
  blocking collectives  401 us (41%)
  local copies, waits for them, and re-layouts  48.3 us (5%)
  matrix products  31.1 us (3%)
  other arithmetic  26.4 us (3%)
  between operations  14.3 us (1%)
    psum x1, blocking collectives, per_device(): lax.psum((pol_terms[1] * jnp.exp(pol_terms[0] - peaks[0]), pol_terms[2],...  246 us
    psum x1, waiting for transfers between devices, per_device(): mixed = lax.psum(partials, 'mdl')  202 us
    ppermute x2, waiting for transfers between devices, gather_around(): earlier.append(lax.ppermute(earlier[-1], axis, up))  175 us
    pmax x2, blocking collectives, per_device(): peaks = lax.pmax(lax.pmax((pol_terms[0], ref_terms[0]), 'mdl'), 'grp')  142 us
    all_gather x1, waiting for transfers between devices, per_device(): lax.all_gather(jnp.stack([pol_hidden, ref_hidden]), 'mdl', axis=1, tiled=...  81.7 us
    unnamed x45, local copies, waits for them, and re-layouts  26.7 us
  transfers between devices with their start and end apart: 5, of which 4 were waited for; matrix products, arithmetic and copies ran while one was open for 2% of the time, Pallas kernels for 0%

profile of v1, /device:TPU:8, one launch (start us, length us, event | category | flops | bytes accessed | tf_op | source)
XLA Modules:
  0.0 983.7 jit_solution(6969346762227151689)
XLA Ops:
  11.0 81.7 %all-gather.2.cloned.1.call-done = bf16[2,256,4096]{2,0,1:T(2,128)(2,1)} async-done(((bf16[2,4,4096]{2,0,1:T(2,128)(2,1)}), bf16[2,256,4096]{2,0,1:T(2,128)(2,1)}) %all-gather.2.cloned.1.call-update) | async-done | bytes 4194320 | tf_op jit(solution)/shard_map/all_gather | solution.py:73
  92.7 13.2 %fusion.50 = (bf16[1,256,4096]{2,0,1:T(2,128)(2,1)S(1)}, bf16[1,256,4096]{2,0,1:T(2,128)(2,1)S(1)}) fusion(bf16[2,256,4096]{2,0,1:T(2,128)(2,1)} %all-gather.2.cloned.1.call-done), kind=kLoop, calls=%fused_computation.86 | loop fusion | bytes 8388608 | tf_op jit(solution)/shard_map/slice | solution.py:79
  105.9 6.7 fusion.8
  115.5 6.6 fusion.21
  122.1 3.7 fusion.26
  125.8 6.6 fusion.20
  133.1 202.1 %all-reduce.7.cloned.1.call-done = (f32[256,4096]{1,0:T(8,128)}, f32[256,4096]{1,0:T(8,128)}) async-done(((f32[256,4096]{1,0:T(8,128)}, f32[256,4096]{1,0:T(8,128)}), (f32[256,4096]{1,0:T(8,128)}, f32[256,4096]{1,0:T(8,128)})) %all-reduce.7.cloned.1.call-update) | async-done | bytes 8388624 | tf_op jit(solution)/shard_map/psum | solution.py:78
  335.2 4.0 fusion.2
  342.8 2.6 pad_maximum_fusion
  346.9 89.7 %collective-permute-done = bf16[2,256,4096]{2,1,0:T(8,128)(2,1)} collective-permute-done((bf16[2,256,4096]{2,1,0:T(8,128)(2,1)}, bf16[2,256,4096]{2,1,0:T(8,128)(2,1)}, u32[]{:S(2)}, u32[]{:S(2)}) %collective-permute-start) | collective-permute-done | bytes 4194336 | tf_op jit(solution)/shard_map/ppermute | solution.py:13
  441.9 85.0 %collective-permute-done.1 = bf16[2,256,4096]{2,1,0:T(8,128)(2,1)} collective-permute-done((bf16[2,256,4096]{2,1,0:T(8,128)(2,1)}, bf16[2,256,4096]{2,1,0:T(8,128)(2,1)}, u32[]{:S(2)}, u32[]{:S(2)}) %collective-permute-start.1) | collective-permute-done | bytes 4194336 | tf_op jit(solution)/shard_map/ppermute | solution.py:13
  526.9 4.8 constant_dynamic-update-slice_fusion.7
  531.7 4.8 constant_dynamic-update-slice_fusion.6
  538.9 4.8 constant_dynamic-update-slice_fusion.4
  543.6 4.9 constant_dynamic-update-slice_fusion.3
  548.5 4.7 constant_dynamic-update-slice_fusion.2
  553.2 2.4 constant_dynamic-update-slice_fusion.1
  555.6 4.7 constant_dynamic-update-slice_fusion
  560.3 5.9 fusion.51
  566.2 6.7 fusion.52
  573.0 131.3 %all-reduce.2 = (f32[1024]{0:T(1024)S(1)}, f32[1024]{0:T(1024)S(1)}) all-reduce(f32[1024]{0:T(1024)S(1)} %get-tuple-element.35, f32[1024]{0:T(1024)S(1)} %get-tuple-element.33), channel_id=1, replica_groups=mesh['grp'=4,'mdl'=64] {'mdl'}, use_global_device_ids=true, to_apply=%region_21.22 | all-reduce | flops 2048 | bytes 16384 | tf_op jit(solution)/shard_map/pmax | solution.py:88
  704.3 10.5 %all-reduce.4 = (f32[1024]{0:T(1024)S(1)}, f32[1024]{0:T(1024)S(1)}) all-reduce(f32[1024]{0:T(1024)S(1)} %get-tuple-element.15, f32[1024]{0:T(1024)S(1)} %get-tuple-element.16), channel_id=1, replica_groups=mesh['grp'=4,'mdl'=64] {'grp'}, use_global_device_ids=true, to_apply=%region_22.23 | all-reduce | flops 2048 | bytes 16384 | tf_op jit(solution)/shard_map/pmax | solution.py:88
  716.5 246.2 %all-reduce = (f32[1024]{0:T(1024)S(1)}, f32[1024]{0:T(1024)S(1)}, f32[1024]{0:T(1024)S(1)}, f32[1024]{0:T(1024)S(1)}) all-reduce(f32[1024]{0:T(1024)S(1)} %exponential_multiply_fusion, f32[1024]{0:T(1024)S(1)} %get-tuple-element.8, f32[1024]{0:T(1024)S(1)} %exponential_multiply_fusion.1, ...), channel_id=1, replica_groups=mesh['grp'=4,'mdl'=64] {'mdl'}, use_global_device_ids=true, to_apply=%region_24.25 | all-reduce | flops 4096 | bytes 32768 | tf_op jit(solution)/shard_map/psum | solution.py:90
  962.7 13.5 %all-reduce.3 = (f32[1024]{0:T(1024)S(1)}, f32[1024]{0:T(1024)S(1)}, f32[1024]{0:T(1024)S(1)}, f32[1024]{0:T(1024)S(1)}) all-reduce(f32[1024]{0:T(1024)S(1)} %get-tuple-element.9, f32[1024]{0:T(1024)S(1)} %get-tuple-element.10, f32[1024]{0:T(1024)S(1)} %get-tuple-element.11, ...), channel_id=1, replica_groups=mesh['grp'=4,'mdl'=64] {'grp'}, use_global_device_ids=true, to_apply=%region_25.26 | all-reduce | flops 4096 | bytes 32768 | tf_op jit(solution)/shard_map/psum | solution.py:89
  (75 shorter events, 22.4 us)
Async XLA Ops:
  7.2 553.1 %copy-start = (bf16[250,4096]{1,0:T(8,128)(2,1)S(1)}, bf16[250,4096]{1,0:T(8,128)(2,1)}, u32[]{:S(2)}) copy-start(bf16[250,4096]{1,0:T(8,128)(2,1)} %param.28) | copy-start | bytes 6144004
  7.2 85.5 %all-gather.2.cloned.1.call-start = ((), (), s32[]{:S(2)}) async-start(), calls=%async_computation | async-start | bytes 4259840 | tf_op jit(solution)/shard_map/all_gather | solution.py:73
  8.9 326.3 %all-reduce.7.cloned.1.call-start = ((), (), s32[]{:S(2)}) async-start(), calls=%async_computation.1 | async-start | bytes 16777216 | tf_op jit(solution)/shard_map/psum | solution.py:78
  105.9 8.0 copy-start.12
  105.9 8.0 copy-start.19
  112.6 1.3 copy-start.6
  112.6 2.9 copy-start.10
  112.6 1.3 copy-start.16
  122.1 3.7 copy-start.11
  132.4 0.7 copy-start.14
  335.2 4.0 copy-start.5
  335.2 4.7 copy-start.9
  339.2 2.9 copy-start.7
  340.8 1.3 copy-start.8
  342.1 3.2 copy-start.1
  342.8 2.6 copy-start.3
  342.8 95.8 %copy-start.17 = (s32[16]{0:T(128)S(1)}, s32[16]{0:T(128)}, u32[]{:S(2)}) copy-start(s32[16]{0:T(128)} %param.31) | copy-start | bytes 196
  345.4 91.2 %collective-permute-start = (bf16[2,256,4096]{2,1,0:T(8,128)(2,1)}, bf16[2,256,4096]{2,1,0:T(8,128)(2,1)}, u32[]{:S(2)}, u32[]{:S(2)}) collective-permute-start(bf16[2,256,4096]{2,1,0:T(8,128)(2,1)} %pad_maximum_fusion), channel_id=1, source_target_pairs={{0,64},{64,128},{128,192},{192,0},{1,65},{65,129},{129,193},{193,1... | collective-permute-start | bytes 12582920 | tf_op jit(solution)/shard_map/ppermute | solution.py:13
  436.6 90.3 %collective-permute-start.1 = (bf16[2,256,4096]{2,1,0:T(8,128)(2,1)}, bf16[2,256,4096]{2,1,0:T(8,128)(2,1)}, u32[]{:S(2)}, u32[]{:S(2)}) collective-permute-start(bf16[2,256,4096]{2,1,0:T(8,128)(2,1)} %collective-permute-done), channel_id=1, source_target_pairs={{0,64},{64,128},{128,192},{192,0},{1,65},{65,129},{129,193},{193,1... | collective-permute-start | bytes 12582920 | tf_op jit(solution)/shard_map/ppermute | solution.py:13
  438.1 100.8 %collective-permute-start.2 = (bf16[2,256,4096]{2,1,0:T(8,128)(2,1)}, bf16[2,256,4096]{2,1,0:T(8,128)(2,1)}, u32[]{:S(2)}, u32[]{:S(2)}) collective-permute-start(bf16[2,256,4096]{2,1,0:T(8,128)(2,1)} %pad_maximum_fusion), channel_id=1, source_target_pairs={{0,192},{64,0},{128,64},{192,128},{1,193},{65,1},{129,65},{193,129... | collective-permute-start | bytes 12582920 | tf_op jit(solution)/shard_map/ppermute | solution.py:15
  531.7 4.8 copy-start.2
  531.7 4.8 copy-start.4
  560.3 5.9 copy-start.18
  566.2 148.5 %copy-start.15 = (s32[1024]{0:T(1024)S(1)}, s32[1024]{0:T(1024)}, u32[]{:S(2)}) copy-start(s32[1024]{0:T(1024)} %param.30) | copy-start | bytes 12292
  (1 other events, 0.7 us)
Sparse Core Ops, SparseCore 0:
  10.8 81.8 all-gather.1
  132.5 202.6 all-reduce.6
